TPU v7x, 256 devices: a whole 4x4x8 slice. The times are simulated.
256 devices in a mesh: seq: 32 (over y, x, core), dev: 8 (over z).
Axes of the slice: x: 4, y: 4, z: 8, core: 2. Of those that a mesh axis runs over, the one named last changes fastest.
Arguments:
- queries: bfloat16 [2048, 4096], P('seq', 'dev'), may hold values from -6 to 6
- key_vectors: bfloat16 [2048, 4096], P('seq', 'dev'), may hold values from -6 to 6
- value_vectors: bfloat16 [2048, 4096], P('seq', 'dev'), may hold values from -6 to 6
- log_decay: float32 [2048, 32], P('seq', 'dev')
- head_gain: float32 [4096], P('dev'), may hold values from 0.5 to 1.5
- gate_weight: bfloat16 [8, 4096, 4096], P('dev', None, 'seq'), may hold values from -0.09375 to 0.09375
- up_weight: bfloat16 [8, 4096, 4096], P('dev', None, 'seq'), may hold values from -0.09375 to 0.09375
- down_weight: bfloat16 [8, 4096, 4096], P('dev', 'seq'), may hold values from -0.0625 to 0.0625
- expert_ids: int32 [2048, 2], P(('seq', 'dev')), may hold values from 0 to 3, all different within a row; in each aligned block of 8 rows (0 to 7, 8 to 15, ...) at most 6 rows name the same one
- expert_weights: float32 [2048, 2], P(('seq', 'dev')), may hold values from 0.2 to 1
Outputs:
- layer_output: bfloat16 [2048, 4096], P(('seq', 'dev'))
Inputs may be any that keep to these rules, and one draw needn't show every extreme that they name: `expert_ids`: in each aligned block of 8 rows (the tokens of one device) no expert is named by more than 6 rows, a bound that some block reaches; the two experts of a row differ.
All inputs are finite; a program needn't handle non-finite values.
Results may differ from a plain program's by a relative error of at most 0.03.
Values may be sent and summed in bfloat16 or wider, within the bound.
No kernel may reach another device: no remote copies, remote signals or barrier semaphores. Data moves between devices by JAX's collectives and lax.ppermute only.
A program may use at most 128 MiB of HBM per device.

v0:
```python
import jax
import jax.numpy as jnp
from jax import lax
from jax.sharding import PartitionSpec as P

PAIR = 2
BLOCK_MAX = 512
highest = lax.Precision.HIGHEST


def carried_in(value, axis, join, neutral):
    place = lax.axis_index(axis)
    gathered = jax.tree.map(
        lambda a, kind: lax.all_gather(a.astype(kind), axis), value, (jnp.bfloat16, jnp.bfloat16)
    )
    state = jax.tree.map(lambda a, e: jnp.zeros_like(a) + jnp.asarray(e, a.dtype), value, neutral)

    def one(turn, state):
        return join(
            state,
            jax.tree.map(
                lambda a, own: lax.dynamic_index_in_dim(a, turn, 0, False).astype(own.dtype),
                gathered,
                value,
            ),
        )

    return lax.fori_loop(0, place, one, state)


def block_step(state, pieces):
    queries_blk, keys_blk, values_blk, decay_blk = pieces
    length = decay_blk.shape[0]
    running = jnp.cumsum(decay_blk)
    causal = jnp.arange(length)[:, None] >= jnp.arange(length)[None, :]
    spread = jnp.where(causal, running[:, None] - running[None, :], 0.0)
    factors = jnp.where(causal, jnp.exp(spread), 0.0)
    scores = jnp.dot(queries_blk, keys_blk.T, preferred_element_type=jnp.float32) * factors
    values_f = values_blk.astype(jnp.float32)
    keys_f = keys_blk.astype(jnp.float32)
    carried = jnp.exp(running)[:, None] * jnp.dot(
        queries_blk.astype(jnp.float32), state, precision=highest
    )
    output = jnp.dot(scores, values_f, precision=highest) + carried
    tail_decay = jnp.exp(running[-1] - running)
    state = jnp.exp(running[-1]) * state + jnp.dot(
        (keys_f * tail_decay[:, None]).T, values_f, precision=highest
    )
    return (state, output)


def run_blocks(state, queries_b, keys_b, values_b, decay_f, block):
    count = decay_f.shape[0] // block
    shaped = (
        queries_b.reshape(count, block, -1),
        keys_b.reshape(count, block, -1),
        values_b.reshape(count, block, -1),
        decay_f.reshape(count, block),
    )
    state, outputs = lax.scan(block_step, state, shaped)
    return outputs.reshape(count * block, -1)


def head_norm(attention, gain):
    square_mean = jnp.mean(attention * attention, axis=-1, keepdims=True)
    return (attention * lax.rsqrt(square_mean + 1e-06) * gain).astype(jnp.bfloat16)


def slot_ranks(flat_experts, experts):
    onehot = (flat_experts[..., None] == jnp.arange(experts, dtype=jnp.int32)).astype(jnp.int32)
    before = jnp.cumsum(onehot, axis=-2) - onehot
    return jnp.sum(before * onehot, axis=-1)


def chain_join(earlier, later):
    return (earlier[0] + later[0], jnp.exp(later[0])[:, None, None] * earlier[1] + later[1])


def per_device(
    queries,
    key_vectors,
    value_vectors,
    log_decay,
    head_gain,
    gate_weight,
    up_weight,
    down_weight,
    expert_ids,
    expert_weights,
):
    seq_len = queries.shape[0]
    heads = log_decay.shape[1]
    head_dim = queries.shape[1] // heads
    queries_h = jnp.transpose(queries.reshape(seq_len, heads, head_dim), (1, 0, 2))
    keys_h = jnp.transpose(key_vectors.reshape(seq_len, heads, head_dim), (1, 0, 2))
    values_h = jnp.transpose(value_vectors.reshape(seq_len, heads, head_dim), (1, 0, 2))
    decay_h = jnp.transpose(log_decay, (1, 0))
    running = jnp.cumsum(decay_h, axis=1)
    log_total = running[:, -1]
    tail_decay = jnp.exp(log_total[:, None] - running)
    local_state = jnp.einsum(
        "hsa,hsb->hab",
        keys_h.astype(jnp.float32) * tail_decay[:, :, None],
        values_h.astype(jnp.float32),
        precision=highest,
    )
    starting = (jnp.zeros((heads,), jnp.float32), jnp.zeros_like(local_state))
    incoming = carried_in((log_total, local_state), "seq", chain_join, starting)[1]
    block = min(BLOCK_MAX, seq_len)

    def one_head(state, head_queries, head_keys, head_values, head_decay):
        return run_blocks(state, head_queries, head_keys, head_values, head_decay, block)

    attention = jax.vmap(one_head)(incoming, queries_h, keys_h, values_h, decay_h)
    normed_h = head_norm(attention, head_gain.reshape(heads, 1, head_dim))
    normed = jnp.transpose(normed_h, (1, 0, 2)).reshape(seq_len, heads * head_dim)
    dev_count = lax.axis_size("dev")
    experts = dev_count // PAIR
    tok_count = expert_ids.shape[0]
    top_count = expert_ids.shape[1]
    capacity = max(2, (3 * tok_count * top_count + 2 * experts - 1) // (2 * experts))
    head_size = normed.shape[1]
    width = head_size * dev_count
    own_flat = expert_ids.reshape(tok_count * top_count)
    own_rank = slot_ranks(own_flat[None, :], experts)[0]
    pick_index = own_flat * capacity + own_rank
    owned_rows = lax.all_to_all(normed, "dev", split_axis=0, concat_axis=1, tiled=True)
    slot_token = (
        jnp.full((experts * capacity,), tok_count, jnp.int32)
        .at[pick_index]
        .set(jnp.arange(tok_count * top_count, dtype=jnp.int32) // top_count)
    )
    padded = jnp.concatenate([owned_rows, jnp.zeros((1, width), owned_rows.dtype)], axis=0)
    send_rows = jnp.repeat(padded[slot_token].reshape(experts, capacity, width), PAIR, axis=0)
    arrived = lax.all_to_all(send_rows, "dev", split_axis=0, concat_axis=0, tiled=True)
    local_rows = arrived.reshape(-1, width)
    piece = lax.all_gather(local_rows, "seq", axis=0, tiled=True)
    gate_part = jnp.dot(piece, gate_weight[0], preferred_element_type=jnp.float32)
    up_part = jnp.dot(piece, up_weight[0], preferred_element_type=jnp.float32)
    hidden_all = (jax.nn.silu(gate_part) * up_part).astype(jnp.bfloat16)
    piece = hidden_all
    term = jnp.dot(piece, down_weight[0], preferred_element_type=jnp.float32).astype(jnp.bfloat16)
    term = lax.optimization_barrier(term)
    summed = lax.psum_scatter(
        term.astype(jnp.float32).astype(jnp.bfloat16), "seq", scatter_dimension=0, tiled=True
    ).astype(jnp.float32)
    returned = lax.all_to_all(
        summed.reshape(dev_count, capacity, width).astype(jnp.bfloat16),
        "dev",
        split_axis=0,
        concat_axis=0,
        tiled=True,
    ).astype(jnp.float32)
    expert_out = jnp.sum(returned.reshape(experts, PAIR, capacity, width), axis=1).astype(
        jnp.bfloat16
    )
    picked = expert_out.reshape(experts * capacity, width)[pick_index].reshape(
        tok_count, top_count, width
    )
    combined = jnp.sum(picked.astype(jnp.float32) * expert_weights[:, :, None], axis=1)
    return combined.astype(jnp.bfloat16)


def solution(mesh):
    in_specs = (
        P("seq", "dev"),
        P("seq", "dev"),
        P("seq", "dev"),
        P("seq", "dev"),
        P("dev"),
        P("dev", None, "seq"),
        P("dev", None, "seq"),
        P("dev", "seq", None),
        P(("seq", "dev"), None),
        P(("seq", "dev"), None),
    )
    out_specs = P(("seq", "dev"), None)
    return jax.shard_map(
        per_device, mesh=mesh, in_specs=in_specs, out_specs=out_specs, check_vma=False
    )
```

profile of v0, /device:TPU:2, one launch (start us, length us, event | category | flops | bytes accessed | tf_op | source)
XLA Modules:
  0.0 384.8 jit_solution(10453502567396986454)
XLA Ops:
  6.5 1.0 reduce_window_sum.25
  7.5 0.2 slice_reduce_fusion
  7.8 2.0 convolution_convert_fusion.1
  9.8 1.3 dynamic-slice.8
  11.7 0.2 fusion.30
  11.9 0.2 dynamic-update-slice
  12.2 62.8 %all-reduce.1 = bf16[128]{0:T(256)(128)(2,1)S(1)} all-reduce(bf16[128]{0:T(256)(128)(2,1)S(1)} %dynamic-update-slice), channel_id=2, replica_groups=mesh['seq'=32,'dev'=8] {'seq'}, use_global_device_ids=true, to_apply=%add.1 | all-reduce | flops 128 | bytes 512
  75.1 0.8 copy.29
  76.0 0.7 broadcast_multiply_fusion
  77.1 0.6 scatter_custom_fusion
  77.7 1.0 convolution_multiply_fusion.1
  78.8 2.2 while.3
  78.9 1.1 convert_add_fusion.2
  80.0 1.0 convert_add_fusion.2
  81.1 1.1 fusion.21
  82.2 1.1 fusion.13
  83.3 0.8 fusion.17
  84.2 0.7 all_to_all.20
  84.9 8.2 %all-to-all-start = ((bf16[8,8,512]{2,1,0:T(8,128)(2,1)}), bf16[8,8,512]{2,1,0:T(8,128)(2,1)S(1)}, u32[]{:S(2)}, u32[]{:S(2)}) async-start(bf16[8,8,512]{2,1,0:T(8,128)(2,1)} %all_to_all.20), calls=%async_computation | async-start | bytes 131072 | tf_op jit(solution)/shard_map/all_to_all | solution.py:127
  93.1 8.3 %all-to-all-done = bf16[8,8,512]{2,1,0:T(8,128)(2,1)S(1)} async-done(((bf16[8,8,512]{2,1,0:T(8,128)(2,1)}), bf16[8,8,512]{2,1,0:T(8,128)(2,1)S(1)}, u32[]{:S(2)}, u32[]{:S(2)}) %all-to-all-start) | async-done | bytes 65568 | tf_op jit(solution)/shard_map/all_to_all | solution.py:127
  101.4 0.7 gather_fusion
  102.2 15.7 %all_to_all.29 = bf16[8,6,4096]{2,1,0:T(8,128)(2,1)S(1)} all-to-all(bf16[8,6,4096]{2,1,0:T(8,128)(2,1)S(1)} %bitcast.114), channel_id=1, replica_groups=mesh['seq'=32,'dev'=8] {'dev'}, dimensions={0} | all-to-all | bytes 786432 | tf_op jit(solution)/shard_map/all_to_all | solution.py:135
  117.9 0.9 reshape.234
  118.9 95.2 %all-gather.5.cloned.1.call-done = bf16[1536,4096]{1,0:T(8,128)(2,1)} async-done(((bf16[48,4096]{1,0:T(8,128)(2,1)}), bf16[1536,4096]{1,0:T(8,128)(2,1)}) %all-gather.5.cloned.1.call-update) | async-done | bytes 12582928 | tf_op jit(solution)/shard_map/all_gather | solution.py:137
  214.2 6.7 %fusion.4 = f32[1536,128]{1,0:T(8,128)S(1)} fusion(bf16[1536,4096]{1,0:T(8,128)(2,1)} %all-gather.5.cloned.1.call-done, bf16[1,4096,128]{2,1,0:T(8,128)(2,1)} %param.17), kind=kOutput, calls=%fused_computation.12 | convolution fusion | flops 1610612736 | bytes 14417920 | tf_op jit(solution)/shard_map/dot_general | solution.py:138
  220.9 18.6 %convolution_convert_fusion = bf16[1536,4096]{1,0:T(8,128)(2,1)} fusion(bf16[1536,4096]{1,0:T(8,128)(2,1)} %all-gather.5.cloned.1.call-done, bf16[1,128,4096]{2,1,0:T(8,128)(2,1)S(1)} %copy-done, bf16[1,4096,128]{2,1,0:T(8,128)(2,1)S(1)} %copy-done.1, f32[1536,128]{1,0:T(8,128)S(1)} %fusion.4), kind=kOutput, calls=%fused_computation.5 | convolution fusion | flops 3228696576 | bytes 28049408 | tf_op jit(solution)/shard_map/dot_general | solution.py:142
  239.5 111.4 %reduce-scatter.2.cloned.1.call-done = bf16[48,4096]{1,0:T(8,128)(2,1)} async-done(((bf16[1536,4096]{1,0:T(8,128)(2,1)}), bf16[48,4096]{1,0:T(8,128)(2,1)}) %reduce-scatter.2.cloned.1.call-update) | async-done | bytes 393232 | tf_op jit(solution)/shard_map/reduce_scatter | solution.py:144
  350.9 1.9 convert_element_type.99
  352.8 7.0 %all-to-all-start.2 = ((bf16[8,6,4096]{2,1,0:T(8,128)(2,1)}), bf16[8,6,4096]{2,1,0:T(8,128)(2,1)S(1)}, u32[]{:S(2)}, u32[]{:S(2)}) async-start(bf16[8,6,4096]{2,1,0:T(8,128)(2,1)} %convert_element_type.99), calls=%async_computation.3 | async-start | bytes 1048576 | tf_op jit(solution)/shard_map/all_to_all | solution.py:147
  360.0 16.3 %all-to-all-done.2 = bf16[8,6,4096]{2,1,0:T(8,128)(2,1)S(1)} async-done(((bf16[8,6,4096]{2,1,0:T(8,128)(2,1)}), bf16[8,6,4096]{2,1,0:T(8,128)(2,1)S(1)}, u32[]{:S(2)}, u32[]{:S(2)}) %all-to-all-start.2) | async-done | bytes 393248 | tf_op jit(solution)/shard_map/all_to_all | solution.py:147
  376.5 0.6 gather_fusion.1
  377.3 1.0 multiply_reduce_fusion
  (40 shorter events, 1.6 us)
Async XLA Ops:
  6.5 214.3 %copy-start = (bf16[1,128,4096]{2,1,0:T(8,128)(2,1)S(1)}, bf16[1,128,4096]{2,1,0:T(8,128)(2,1)}, u32[]{:S(2)}) copy-start(bf16[1,128,4096]{2,1,0:T(8,128)(2,1)} %param.19) | copy-start | bytes 3145732
  6.5 72.3 %all-gather.7.cloned.1.call-start = ((), (), s32[]{:S(2)}) async-start(), calls=%async_computation.6 | async-start | bytes 4325376 | tf_op jit(solution)/shard_map/all_gather | solution.py:14
  78.8 142.0 %copy-start.1 = (bf16[1,4096,128]{2,1,0:T(8,128)(2,1)S(1)}, bf16[1,4096,128]{2,1,0:T(8,128)(2,1)}, u32[]{:S(2)}) copy-start(bf16[1,4096,128]{2,1,0:T(8,128)(2,1)} %param.18) | copy-start | bytes 3145732
  84.9 16.6 %all-to-all-start = ((bf16[8,8,512]{2,1,0:T(8,128)(2,1)}), bf16[8,8,512]{2,1,0:T(8,128)(2,1)S(1)}, u32[]{:S(2)}, u32[]{:S(2)}) async-start(bf16[8,8,512]{2,1,0:T(8,128)(2,1)} %all_to_all.20), calls=%async_computation | async-start | bytes 131072 | tf_op jit(solution)/shard_map/all_to_all | solution.py:127
  93.1 121.1 %all-gather.5.cloned.1.call-start = ((), (), s32[]{:S(2)}) async-start(), calls=%async_computation.4 | async-start | bytes 12976128 | tf_op jit(solution)/shard_map/all_gather | solution.py:137
  118.9 232.0 %reduce-scatter.2.cloned.1.call-start = ((), (), s32[]{:S(2)}) async-start(), calls=%async_computation.5 | async-start | bytes 12976128 | tf_op jit(solution)/shard_map/reduce_scatter | solution.py:144
  239.5 120.4 %copy-start.2 = (f32[8,2]{0,1:T(2,128)S(1)}, f32[8,2]{0,1:T(2,128)}, u32[]{:S(2)}) copy-start(f32[8,2]{0,1:T(2,128)} %param.21) | copy-start | bytes 196
  352.8 23.4 %all-to-all-start.2 = ((bf16[8,6,4096]{2,1,0:T(8,128)(2,1)}), bf16[8,6,4096]{2,1,0:T(8,128)(2,1)S(1)}, u32[]{:S(2)}, u32[]{:S(2)}) async-start(bf16[8,6,4096]{2,1,0:T(8,128)(2,1)} %convert_element_type.99), calls=%async_computation.3 | async-start | bytes 1048576 | tf_op jit(solution)/shard_map/all_to_all | solution.py:147
Sparse Core Ops, SparseCore 0:
  9.9 53.7 all-gather.6
  119.0 95.1 all-gather.4
  239.6 111.2 reduce-scatter.1
where the time goes:
time: 386 us; the launch traced here: 385 us
  waiting for transfers between devices  231 us (60%)
  blocking collectives  78.5 us (20%)
  matrix products  30.5 us (8%)
  starting transfers between devices  15.3 us (4%)
  between operations  14 us (4%)
  local copies, waits for them, and re-layouts  8.93 us (2%)
  other arithmetic  6.19 us (2%)
    reduce_scatter x1, waiting for transfers between devices, per_device(): lax.psum_scatter(term.astype(jnp.float32).astype(jnp.bfloat16), 'seq', sc...  111 us
    all_gather x1, waiting for transfers between devices, per_device(): piece = lax.all_gather(local_rows, 'seq', axis=0, tiled=True)  95.2 us
    unnamed x1, blocking collectives  62.8 us
    dot_general x1, matrix products, per_device(): jnp.dot(piece, down_weight[0], preferred_element_type=jnp.float32)  18.6 us
    all_to_all x1, waiting for transfers between devices, per_device(): lax.all_to_all(summed.reshape(dev_count, capacity, width).astype(jnp.bflo...  16.3 us
    all_to_all x1, blocking collectives, per_device(): lax.all_to_all(send_rows, 'dev', split_axis=0, concat_axis=0, tiled=True)  15.7 us
    all_to_all x1, waiting for transfers between devices, per_device(): lax.all_to_all(normed, 'dev', split_axis=0, concat_axis=1, tiled=True)  8.31 us
    all_to_all x1, starting transfers between devices, per_device(): lax.all_to_all(normed, 'dev', split_axis=0, concat_axis=1, tiled=True)  8.19 us
  transfers between devices with their start and end apart: 5, of which 4 were waited for; matrix products, arithmetic and copies ran while one was open for 1% of the time, Pallas kernels for 0%

commit v1 on v0

--- a/solution.py
+++ b/solution.py
@@ -134,7 +134,9 @@
     send_rows = jnp.repeat(padded[slot_token].reshape(experts, capacity, width), PAIR, axis=0)
     arrived = lax.all_to_all(send_rows, "dev", split_axis=0, concat_axis=0, tiled=True)
     local_rows = arrived.reshape(-1, width)
-    piece = lax.all_gather(local_rows, "seq", axis=0, tiled=True)
+    piece = jnp.concatenate(
+        lax.all_to_all(jnp.stack([local_rows] * lax.axis_size("seq")), "seq", 0, 0), axis=0
+    )
     gate_part = jnp.dot(piece, gate_weight[0], preferred_element_type=jnp.float32)
     up_part = jnp.dot(piece, up_weight[0], preferred_element_type=jnp.float32)
     hidden_all = (jax.nn.silu(gate_part) * up_part).astype(jnp.bfloat16)

time: 386 us -> 472 us (1.22)
  blocking collectives: 78.5 us -> 257 us
  waiting for transfers between devices: 231 us -> 132 us
  local copies, waits for them, and re-layouts: 8.93 us -> 18.8 us
    all_to_all x0 -> x1, blocking collectives: none -> 178 us  [per_device(): lax.all_to_all(jnp.stack([local_rows] * lax.axis_size('seq')), 'seq', 0, 0)]
    all_gather x1 -> x0, waiting for transfers between devices: 95.2 us -> none  [per_device(): piece = lax.all_gather(local_rows, 'seq', axis=0, tiled=True)]
    another operation x0 -> x2, local copies, waits for them, and re-layouts: none -> 6.29 us  [per_device(): jnp.stack([local_rows] * lax.axis_size('seq'))]
  transfers between devices with their start and end apart: 5 -> 4, of which waited for: 4 -> 3; matrix products, arithmetic and copies ran while one was open for 1% -> 1% of each run, Pallas kernels for 0% -> 0%
where the time goes in v1:
time: 472 us; the launch traced here: 471 us
  blocking collectives  257 us (54%)
  waiting for transfers between devices  132 us (28%)
  matrix products  27.3 us (6%)
  local copies, waits for them, and re-layouts  18.8 us (4%)
  starting transfers between devices  15.2 us (3%)
  between operations  14.3 us (3%)
  other arithmetic  6.12 us (1%)
    all_to_all x1, blocking collectives, per_device(): lax.all_to_all(jnp.stack([local_rows] * lax.axis_size('seq')), 'seq', 0, 0)  178 us
    reduce_scatter x1, waiting for transfers between devices, per_device(): lax.psum_scatter(term.astype(jnp.float32).astype(jnp.bfloat16), 'seq', sc...  108 us
    unnamed x1, blocking collectives  62.8 us
    dot_general x1, matrix products, per_device(): jnp.dot(piece, down_weight[0], preferred_element_type=jnp.float32)  18.6 us
    all_to_all x1, waiting for transfers between devices, per_device(): lax.all_to_all(summed.reshape(dev_count, capacity, width).astype(jnp.bflo...  16.3 us
    all_to_all x1, blocking collectives, per_device(): lax.all_to_all(send_rows, 'dev', split_axis=0, concat_axis=0, tiled=True)  15.7 us
  transfers between devices with their start and end apart: 4, of which 3 were waited for; matrix products, arithmetic and copies ran while one was open for 1% of the time, Pallas kernels for 0%

profile of v1, /device:TPU:2, one launch (start us, length us, event | category | flops | bytes accessed | tf_op | source)
XLA Modules:
  0.0 471.1 jit_solution(11929414708672251249)
XLA Ops:
  6.5 1.0 reduce_window_sum.25
  7.5 0.2 slice_reduce_fusion
  7.8 2.0 convolution_convert_fusion.1
  9.8 1.3 dynamic-slice.8
  11.9 0.2 dynamic-update-slice
  12.2 62.8 %all-reduce.1 = bf16[128]{0:T(256)(128)(2,1)S(1)} all-reduce(bf16[128]{0:T(256)(128)(2,1)S(1)} %dynamic-update-slice), channel_id=2, replica_groups=mesh['seq'=32,'dev'=8] {'seq'}, use_global_device_ids=true, to_apply=%add.1 | all-reduce | flops 128 | bytes 512
  75.1 0.8 copy.29
  76.0 0.7 broadcast_multiply_fusion
  77.1 0.6 scatter_custom_fusion
  77.7 1.0 convolution_multiply_fusion.1
  78.8 2.1 while.3
  78.9 1.0 convert_add_fusion.2
  79.9 1.0 convert_add_fusion.2
  81.0 1.1 fusion.21
  82.1 1.1 fusion.13
  83.2 0.8 fusion.17
  84.1 0.7 all_to_all.23
  84.8 8.2 %all-to-all-start = ((bf16[8,8,512]{2,1,0:T(8,128)(2,1)}), bf16[8,8,512]{2,1,0:T(8,128)(2,1)S(1)}, u32[]{:S(2)}, u32[]{:S(2)}) async-start(bf16[8,8,512]{2,1,0:T(8,128)(2,1)} %all_to_all.23), calls=%async_computation | async-start | bytes 131072 | tf_op jit(solution)/shard_map/all_to_all | solution.py:127
  93.0 8.3 %all-to-all-done = bf16[8,8,512]{2,1,0:T(8,128)(2,1)S(1)} async-done(((bf16[8,8,512]{2,1,0:T(8,128)(2,1)}), bf16[8,8,512]{2,1,0:T(8,128)(2,1)S(1)}, u32[]{:S(2)}, u32[]{:S(2)}) %all-to-all-start) | async-done | bytes 65568 | tf_op jit(solution)/shard_map/all_to_all | solution.py:127
  101.4 0.7 gather_fusion
  102.2 15.7 %all_to_all.34 = bf16[8,6,4096]{2,1,0:T(8,128)(2,1)S(1)} all-to-all(bf16[8,6,4096]{2,1,0:T(8,128)(2,1)S(1)} %bitcast.117), channel_id=1, replica_groups=mesh['seq'=32,'dev'=8] {'dev'}, dimensions={0} | all-to-all | bytes 786432 | tf_op jit(solution)/shard_map/all_to_all | solution.py:135
  118.0 6.2 %stack.3 = bf16[32,48,4096]{2,1,0:T(8,128)(2,1)} broadcast(bf16[48,4096]{1,0:T(8,128)(2,1)S(1)} %stack_reshape.2), dimensions={1,2} | broadcast | bytes 12976128 | tf_op jit(solution)/shard_map/stack | solution.py:138
  124.2 178.4 %all_to_all.35 = bf16[32,48,4096]{2,1,0:T(8,128)(2,1)S(1)} all-to-all(bf16[32,48,4096]{2,1,0:T(8,128)(2,1)} %stack.3), channel_id=1, replica_groups=mesh['seq'=32,'dev'=8] {'seq'}, dimensions={0} | all-to-all | bytes 25165824 | tf_op jit(solution)/shard_map/all_to_all | solution.py:138
  302.5 4.5 copy-done.1
  307.0 3.4 fusion.4
  310.5 18.6 %convolution_convert_fusion = bf16[1536,4096]{1,0:T(8,128)(2,1)} fusion(bf16[1536,4096]{1,0:T(8,128)(2,1)} %bitcast.116, bf16[1,128,4096]{2,1,0:T(8,128)(2,1)S(1)} %copy-done, bf16[1,4096,128]{2,1,0:T(8,128)(2,1)S(1)} %copy-done.2, f32[1536,128]{1,0:T(8,128)S(1)} %fusion.4), kind=kOutput, calls=%fused_computation.5 | convolution fusion | flops 3228696576 | bytes 28049408 | tf_op jit(solution)/shard_map/dot_general | solution.py:144
  329.1 107.7 %reduce-scatter.2.cloned.1.call-done = bf16[48,4096]{1,0:T(8,128)(2,1)} async-done(((bf16[1536,4096]{1,0:T(8,128)(2,1)}), bf16[48,4096]{1,0:T(8,128)(2,1)}) %reduce-scatter.2.cloned.1.call-update) | async-done | bytes 393232 | tf_op jit(solution)/shard_map/reduce_scatter | solution.py:146
  436.9 1.9 convert_element_type.99
  438.8 7.0 %all-to-all-start.3 = ((bf16[8,6,4096]{2,1,0:T(8,128)(2,1)}), bf16[8,6,4096]{2,1,0:T(8,128)(2,1)S(1)}, u32[]{:S(2)}, u32[]{:S(2)}) async-start(bf16[8,6,4096]{2,1,0:T(8,128)(2,1)} %convert_element_type.99), calls=%async_computation.4 | async-start | bytes 1048576 | tf_op jit(solution)/shard_map/all_to_all | solution.py:149
  445.9 16.3 %all-to-all-done.3 = bf16[8,6,4096]{2,1,0:T(8,128)(2,1)S(1)} async-done(((bf16[8,6,4096]{2,1,0:T(8,128)(2,1)}), bf16[8,6,4096]{2,1,0:T(8,128)(2,1)S(1)}, u32[]{:S(2)}, u32[]{:S(2)}) %all-to-all-start.3) | async-done | bytes 393248 | tf_op jit(solution)/shard_map/all_to_all | solution.py:149
  462.4 0.6 gather_fusion.1
  463.2 1.0 multiply_reduce_fusion
  (43 shorter events, 1.8 us)
Async XLA Ops:
  6.5 303.9 %copy-start = (bf16[1,128,4096]{2,1,0:T(8,128)(2,1)S(1)}, bf16[1,128,4096]{2,1,0:T(8,128)(2,1)}, u32[]{:S(2)}) copy-start(bf16[1,128,4096]{2,1,0:T(8,128)(2,1)} %param.19) | copy-start | bytes 3145732
  6.5 72.3 %all-gather.4.cloned.1.call-start = ((), (), s32[]{:S(2)}) async-start(), calls=%async_computation.6 | async-start | bytes 4325376 | tf_op jit(solution)/shard_map/all_gather | solution.py:14
  84.8 16.6 %all-to-all-start = ((bf16[8,8,512]{2,1,0:T(8,128)(2,1)}), bf16[8,8,512]{2,1,0:T(8,128)(2,1)S(1)}, u32[]{:S(2)}, u32[]{:S(2)}) async-start(bf16[8,8,512]{2,1,0:T(8,128)(2,1)} %all_to_all.23), calls=%async_computation | async-start | bytes 131072 | tf_op jit(solution)/shard_map/all_to_all | solution.py:127
  93.0 343.9 %reduce-scatter.2.cloned.1.call-start = ((), (), s32[]{:S(2)}) async-start(), calls=%async_computation.5 | async-start | bytes 12976128 | tf_op jit(solution)/shard_map/reduce_scatter | solution.py:146
  124.1 182.9 %copy-start.4 = (bf16[1,4096,128]{2,1,0:T(8,128)(2,1)S(1)}, bf16[1,4096,128]{2,1,0:T(8,128)(2,1)}, u32[]{:S(2)}) copy-start(bf16[1,4096,128]{2,1,0:T(8,128)(2,1)} %param.17) | copy-start | bytes 3145732
  302.5 4.5 copy-start.1
  302.5 8.0 %copy-start.2 = (bf16[1,4096,128]{2,1,0:T(8,128)(2,1)S(1)}, bf16[1,4096,128]{2,1,0:T(8,128)(2,1)}, u32[]{:S(2)}) copy-start(bf16[1,4096,128]{2,1,0:T(8,128)(2,1)} %param.18) | copy-start | bytes 3145732
  329.1 116.7 %copy-start.3 = (f32[8,2]{0,1:T(2,128)S(1)}, f32[8,2]{0,1:T(2,128)}, u32[]{:S(2)}) copy-start(f32[8,2]{0,1:T(2,128)} %param.21) | copy-start | bytes 196
  438.8 23.4 %all-to-all-start.3 = ((bf16[8,6,4096]{2,1,0:T(8,128)(2,1)}), bf16[8,6,4096]{2,1,0:T(8,128)(2,1)S(1)}, u32[]{:S(2)}, u32[]{:S(2)}) async-start(bf16[8,6,4096]{2,1,0:T(8,128)(2,1)} %convert_element_type.99), calls=%async_computation.4 | async-start | bytes 1048576 | tf_op jit(solution)/shard_map/all_to_all | solution.py:149
Sparse Core Ops, SparseCore 0:
  9.9 53.7 all-gather.3
  329.3 107.5 reduce-scatter.1
